TPU v7x, 512 devices: a whole 4x4x16 slice. The times are simulated.
512 devices in a mesh: dp: 16 (over z), row: 4 (over y), col: 8 (over x, core).
Axes of the slice: x: 4, y: 4, z: 16, core: 2. Of those that a mesh axis runs over, the one named last changes fastest.
Arguments:
- layer_input: bfloat16 [3072, 4096], P(('dp', 'col'), 'row'), may hold values from -6 to 6
- hidden_grad: bfloat16 [3072, 14336], P(('dp', 'row'), 'col'), may hold values from -6 to 6
- gate_slots: bfloat16 [4, 8, 48, 128, 128], P('row', 'col', 'dp'), may hold values from -0.125 to 0.125
- up_slots: bfloat16 [4, 8, 48, 128, 128], P('row', 'col', 'dp'), may hold values from -0.125 to 0.125
- block_mask: int32 [32, 112], replicated, may hold values from 0 to 1, as said below
Outputs:
- input_grad: bfloat16 [3072, 4096], P(('dp', 'col'), 'row')
- gate_slot_grad: float32 [4, 8, 48, 128, 128], P('row', 'col', 'dp')
- up_slot_grad: float32 [4, 8, 48, 128, 128], P('row', 'col', 'dp')
Inputs may be any that keep to these rules, and one draw needn't show every extreme that they name: `block_mask`: every tile of 8 x 14 blocks keeps between 24 and 48 blocks; some tile keeps exactly 48, which tile depends on the draw.
All inputs are finite; a program needn't handle non-finite values.
Results may differ from a plain program's by a relative error of at most 0.022.
Values may be sent and summed in bfloat16 or wider, within the bound.
No kernel may reach another device: no remote copies, remote signals or barrier semaphores. Data moves between devices by JAX's collectives and lax.ppermute only.
A program may use at most 64 MiB of HBM per device.

v0:
```python
import jax
import jax.numpy as jnp
from jax import lax
from jax.sharding import PartitionSpec as P


def slot_maps(block_mask, tile_rows, tile_cols, capacity):
    row_first = lax.axis_index("row") * tile_rows
    col_first = lax.axis_index("col") * tile_cols
    tile_mask = lax.dynamic_slice(block_mask, (row_first, col_first), (tile_rows, tile_cols))
    flat_mask = tile_mask.reshape(tile_rows * tile_cols)
    position = jnp.cumsum(flat_mask) - 1
    slot_ids = jnp.arange(capacity, dtype=jnp.int32)
    chosen = ((flat_mask[:, None] > 0) & (position[:, None] == slot_ids[None, :])).astype(jnp.int32)
    block_ids = jnp.arange(tile_rows * tile_cols, dtype=jnp.int32)
    slot_block = jnp.sum(chosen * block_ids[:, None], axis=0)
    live_slots = jnp.sum(chosen, axis=0).astype(jnp.float32)
    slot_row = slot_block // tile_cols
    slot_col = slot_block % tile_cols
    col_table = (slot_col[:, None] == jnp.arange(tile_cols, dtype=jnp.int32)[None, :]).astype(
        jnp.float32
    ) * live_slots[:, None]
    row_table = (slot_row[:, None] == jnp.arange(tile_rows, dtype=jnp.int32)[None, :]).astype(
        jnp.float32
    ) * live_slots[:, None]
    return (slot_row, slot_col, live_slots, col_table, row_table)


def slot_products(picked, pair_weights, col_table):
    per_slot = jnp.einsum("tsk,skn->tsn", picked, pair_weights, preferred_element_type=jnp.float32)
    return jnp.einsum("tsn,sc->tcn", per_slot, col_table, precision=lax.Precision.HIGHEST)


def back_products(grad_picked, pair_weights, row_table):
    per_slot = jnp.einsum(
        "tsn,skn->tsk", grad_picked, pair_weights, preferred_element_type=jnp.float32
    )
    return jnp.einsum("tsk,sr->trk", per_slot, row_table, precision=lax.Precision.HIGHEST)


def on_device(layer_input, hidden_grad, gate_slots, up_slots, block_mask):
    gate_local = gate_slots[0, 0]
    up_local = up_slots[0, 0]
    block_size = gate_local.shape[-1]
    replicas = lax.axis_size("dp")
    capacity = gate_local.shape[0] * replicas
    token_panel = lax.all_gather(layer_input, "col", axis=0, tiled=True)
    grad_panel = lax.all_gather(hidden_grad, "row", axis=0, tiled=True)
    tok_rows = token_panel.shape[0]
    feat_cols = token_panel.shape[1]
    unit_cols = grad_panel.shape[1]
    tile_rows = feat_cols // block_size
    tile_cols = unit_cols // block_size
    slot_row, slot_col, live_slots, col_table, row_table = slot_maps(
        block_mask, tile_rows, tile_cols, capacity
    )
    token_blocks = token_panel.reshape(tok_rows, tile_rows, block_size)
    picked_tokens = jnp.take(token_blocks, slot_row, axis=1)
    gate_all, up_all = (
        lax.all_gather(gate_local, "dp", axis=0, tiled=True),
        lax.all_gather(up_local, "dp", axis=0, tiled=True),
    )
    pair_all = jnp.concatenate([gate_all, up_all], axis=2)
    pair_part = slot_products(picked_tokens, pair_all, col_table)
    gate_part = pair_part[:, :, :block_size].reshape(tok_rows, unit_cols)
    up_part = pair_part[:, :, block_size:].reshape(tok_rows, unit_cols)
    gate_sum, up_sum = (
        lax.psum(gate_part.astype(jnp.bfloat16), "row").astype(jnp.float32),
        lax.psum(up_part.astype(jnp.bfloat16), "row").astype(jnp.float32),
    )
    sigmoid_gate = jax.nn.sigmoid(gate_sum)
    upstream = grad_panel.astype(jnp.float32)
    gate_grad = (upstream * up_sum * sigmoid_gate * (1.0 + gate_sum * (1.0 - sigmoid_gate))).astype(
        jnp.bfloat16
    )
    up_grad = (upstream * gate_sum * sigmoid_gate).astype(jnp.bfloat16)
    grad_pair = jnp.concatenate(
        [
            gate_grad.reshape(tok_rows, tile_cols, block_size),
            up_grad.reshape(tok_rows, tile_cols, block_size),
        ],
        axis=2,
    )
    grad_picked = jnp.take(grad_pair, slot_col, axis=1)
    summed = back_products(grad_picked, pair_all, row_table)
    input_sum = lax.psum_scatter(
        summed.reshape(tok_rows // lax.axis_size("col") * lax.axis_size("col"), feat_cols).astype(
            jnp.bfloat16
        ),
        "col",
        scatter_dimension=0,
        tiled=True,
    )
    pair_term = (
        jnp.einsum("tsk,tsn->skn", picked_tokens, grad_picked, preferred_element_type=jnp.float32)
        * live_slots[:, None, None]
    )
    pair_total = lax.psum_scatter(
        pair_term.astype(jnp.bfloat16), "dp", scatter_dimension=0, tiled=True
    ).astype(jnp.float32)
    gate_out = (pair_total[:, :, :block_size] / replicas)[None, None]
    up_out = (pair_total[:, :, block_size:] / replicas)[None, None]
    return (input_sum, gate_out, up_out)


def solution(mesh):
    return jax.shard_map(
        on_device,
        mesh=mesh,
        in_specs=(
            P(("dp", "col"), "row"),
            P(("dp", "row"), "col"),
            P("row", "col", "dp", None, None),
            P("row", "col", "dp", None, None),
            P(),
        ),
        out_specs=(
            P(("dp", "col"), "row"),
            P("row", "col", "dp", None, None),
            P("row", "col", "dp", None, None),
        ),
        check_vma=False,
    )
```

profile of v0, /device:TPU:8, one launch (start us, length us, event | category | flops | bytes accessed | tf_op | source)
XLA Modules:
  0.0 370.0 jit_solution(6575437389521833175)
XLA Ops:
  7.2 0.7 all-gather.5.cloned.1.call-update
  7.9 0.7 all-gather.7.cloned.1.call-update
  8.7 0.8 broadcast_compare_fusion
  10.1 13.5 %all_gather.15 = bf16[192,1024]{1,0:T(8,128)(2,1)S(1)} all-gather(bf16[24,1024]{1,0:T(8,128)(2,1)} %param.5), channel_id=1, replica_groups=mesh['dp'=16,'row'=4,'col'=8] {'col'}, dimensions={0}, use_global_device_ids=true | all-gather | bytes 442368 | tf_op jit(solution)/shard_map/all_gather | solution.py:47
  23.7 1.0 gather_fusion
  24.7 61.7 %all-gather.5.cloned.1.call-done = bf16[1,1,48,128,128]{4,3,1,0,2:T(8,128)(2,1)} async-done(((bf16[1,1,3,128,128]{4,3,1,0,2:T(8,128)(2,1)}), bf16[1,1,48,128,128]{4,3,1,0,2:T(8,128)(2,1)}) %all-gather.5.cloned.1.call-update) | async-done | bytes 1572880 | tf_op jit(solution)/shard_map/all_gather | solution.py:60
  86.4 71.1 %all-gather.7.cloned.1.call-done = bf16[1,1,48,128,128]{4,3,1,0,2:T(8,128)(2,1)} async-done(((bf16[1,1,3,128,128]{4,3,1,0,2:T(8,128)(2,1)}), bf16[1,1,48,128,128]{4,3,1,0,2:T(8,128)(2,1)}) %all-gather.7.cloned.1.call-update) | async-done | bytes 1572880 | tf_op jit(solution)/shard_map/all_gather | solution.py:61
  157.5 3.3 convolution_bitcast_fusion
  160.8 9.9 %fusion.20 = bf16[192,14,256]{2,1,0:T(8,128)(2,1)S(1)} fusion(f32[192,48,256]{2,0,1:T(8,128)S(1)} %convolution_bitcast_fusion, f32[48]{0:T(128)S(1)} %convert_element_type.55, s32[48]{0:T(128)S(1)} %get-tuple-element.8), kind=kOutput, calls=%fused_computation.23 | convolution fusion | flops 397051200 | bytes 10813824 | tf_op jit(solution)/shard_map/tsn,sc->tcn/dot_general | solution.py:31
  171.0 1.0 copy.56
  172.1 1.1 copy.57
  173.2 13.2 %all_gather.14 = bf16[192,1792]{1,0:T(8,128)(2,1)S(1)} all-gather(bf16[48,1792]{1,0:T(8,128)(2,1)S(1)} %copy-done.3), channel_id=1, replica_groups=mesh['dp'=16,'row'=4,'col'=8] {'row'}, dimensions={0}, use_global_device_ids=true | all-gather | bytes 860160 | tf_op jit(solution)/shard_map/all_gather | solution.py:48
  186.4 46.7 %all-reduce.3.cloned.1.call-done = (bf16[192,1792]{1,0:T(8,128)(2,1)}, bf16[192,1792]{1,0:T(8,128)(2,1)}) async-done(((bf16[192,1792]{1,0:T(8,128)(2,1)}, bf16[192,1792]{1,0:T(8,128)(2,1)}), (bf16[192,1792]{1,0:T(8,128)(2,1)}, bf16[192,1792]{1,0:T(8,128)(2,1)})) %all-reduce.3.cloned.1.call-update) | async-done | bytes 1376272 | tf_op jit(solution)/shard_map/psum | solution.py:68
  233.1 2.1 fusion.36
  235.7 3.1 gather_fusion.1
  238.8 6.2 %multiply_convert_fusion = bf16[48,128,256]{2,1,0:T(8,128)(2,1)} fusion(f32[48]{0:T(128)S(1)} %convert_element_type.55, bf16[48,192,256]{2,1,0:T(8,128)(2,1)} %gather_fusion.1, pred[48]{0:T(512)(128)(4,1)S(1)} %get-tuple-element.7, bf16[48,192,128]{2,1,0:T(8,128)(2,1)} %copy-done, pred[48]{0:T(512)(128)(4,1)S(1)} %get-tuple-element.22), kind=kOutput, calls=%fused_computation.4 | convolution fusion | flops 610664448 | bytes 10223904 | tf_op jit(solution)/shard_map/tsk,tsn->skn/dot_general | solution.py:95
  245.1 1.3 copy-done.1
  246.9 3.3 fusion.10
  250.3 4.9 %fusion.32 = bf16[8,192,128]{2,0,1:T(8,128)(2,1)S(1)} fusion(f32[192,48,128]{2,0,1:T(8,128)S(1)} %fusion.10, f32[48]{0:T(128)S(1)} %convert_element_type.55, s32[48]{0:T(128)S(1)} %get-tuple-element.23), kind=kOutput, calls=%fused_computation.34 | convolution fusion | flops 113443584 | bytes 5112192 | tf_op jit(solution)/shard_map/tsk,sr->trk/dot_general | solution.py:38
  255.2 0.8 copy.60
  256.0 67.8 %reduce-scatter.5.cloned.1.call-done = bf16[3,128,256]{2,1,0:T(8,128)(2,1)} async-done(((bf16[48,128,256]{2,1,0:T(8,128)(2,1)}), bf16[3,128,256]{2,1,0:T(8,128)(2,1)}) %reduce-scatter.5.cloned.1.call-update) | async-done | bytes 196624 | tf_op jit(solution)/shard_map/reduce_scatter | solution.py:98
  323.8 1.0 convert_element_type.67
  324.8 0.8 fusion.37
  325.5 38.0 %reduce-scatter.3.cloned.1.call-done = bf16[24,1024]{1,0:T(8,128)(2,1)} async-done(((bf16[192,1024]{1,0:T(8,128)(2,1)}), bf16[24,1024]{1,0:T(8,128)(2,1)}) %reduce-scatter.3.cloned.1.call-update) | async-done | bytes 49168 | tf_op jit(solution)/shard_map/reduce_scatter | solution.py:86
  (29 shorter events, 2.2 us)
Async XLA Ops:
  7.2 79.3 %all-gather.5.cloned.1.call-start = ((), (), s32[]{:S(2)}) async-start(), calls=%async_computation.4 | async-start | bytes 1671168 | tf_op jit(solution)/shard_map/all_gather | solution.py:60
  7.9 149.6 %all-gather.7.cloned.1.call-start = ((), (), s32[]{:S(2)}) async-start(), calls=%async_computation.5 | async-start | bytes 1671168 | tf_op jit(solution)/shard_map/all_gather | solution.py:61
  8.6 224.4 %all-reduce.3.cloned.1.call-start = ((), (), s32[]{:S(2)}) async-start(), calls=%async_computation.6 | async-start | bytes 2752512 | tf_op jit(solution)/shard_map/psum | solution.py:68
  24.7 136.1 %copy-start = (bf16[48,192,128]{2,1,0:T(8,128)(2,1)}, bf16[48,192,128]{2,1,0:T(8,128)(2,1)S(1)}, u32[]{:S(2)}) copy-start(bf16[48,192,128]{2,1,0:T(8,128)(2,1)S(1)} %gather_fusion) | copy-start | bytes 7077892
  171.0 2.2 copy-start.3
  173.2 150.6 %reduce-scatter.5.cloned.1.call-start = ((), (), s32[]{:S(2)}) async-start(), calls=%async_computation.3 | async-start | bytes 3342336 | tf_op jit(solution)/shard_map/reduce_scatter | solution.py:98
  245.1 1.4 copy-start.1
  245.1 1.9 copy-start.2
  245.1 118.4 %reduce-scatter.3.cloned.1.call-start = ((), (), s32[]{:S(2)}) async-start(), calls=%async_computation.2 | async-start | bytes 442368 | tf_op jit(solution)/shard_map/reduce_scatter | solution.py:86
Sparse Core Ops, SparseCore 0:
  10.0 76.3 all-gather.4
  88.5 68.9 all-gather.6
  173.3 59.7 all-reduce.2
  245.2 78.5 reduce-scatter.4
  327.0 36.4 reduce-scatter.2
where the time goes:
time: 370 us
  waiting for transfers between devices  287 us (78%)
  matrix products  27.7 us (7%)
  blocking collectives  26.7 us (7%)
  between operations  13.9 us (4%)
  local copies, waits for them, and re-layouts  9.72 us (3%)
  other arithmetic  5.19 us (1%)
    all_gather x1, waiting for transfers between devices, on_device(): lax.all_gather(up_local, 'dp', axis=0, tiled=True)  71.1 us
    reduce_scatter x1, waiting for transfers between devices, on_device(): lax.psum_scatter(pair_term.astype(jnp.bfloat16), 'dp', scatter_dimension=...  67.8 us
    all_gather x1, waiting for transfers between devices, on_device(): lax.all_gather(gate_local, 'dp', axis=0, tiled=True)  61.7 us
    psum x1, waiting for transfers between devices, on_device(): lax.psum(gate_part.astype(jnp.bfloat16), 'row').astype(jnp.float32)  46.7 us
    reduce_scatter x1, waiting for transfers between devices, on_device(): lax.psum_scatter(summed.reshape(tok_rows // lax.axis_size('col') * lax.ax...  38 us
    all_gather x1, blocking collectives, on_device(): token_panel = lax.all_gather(layer_input, 'col', axis=0, tiled=True)  13.5 us
    all_gather x1, blocking collectives, on_device(): grad_panel = lax.all_gather(hidden_grad, 'row', axis=0, tiled=True)  13.2 us
    dot_general x1, matrix products, slot_products(): jnp.einsum('tsn,sc->tcn', per_slot, col_table, precision=lax.Precision.HI...  9.9 us
  transfers between devices with their start and end apart: 5, of which 5 were waited for; matrix products, arithmetic and copies ran while one was open for 4% of the time, Pallas kernels for 0%

commit v1 on v0

--- a/solution.py
+++ b/solution.py
@@ -1,7 +1,16 @@
+import functools
 import jax
 import jax.numpy as jnp
 from jax import lax
 from jax.sharding import PartitionSpec as P
+
+
+def match_block_by_axis(shard_in, shard_axis):
+    taken_in = jnp.sum(lax.all_gather(shard_in, axis_name=shard_axis), 0)
+    return taken_in
+
+
+put_bands = functools.partial(match_block_by_axis, shard_axis="row")
 
 
 def slot_maps(block_mask, tile_rows, tile_cols, capacity):
@@ -65,7 +74,7 @@
     gate_part = pair_part[:, :, :block_size].reshape(tok_rows, unit_cols)
     up_part = pair_part[:, :, block_size:].reshape(tok_rows, unit_cols)
     gate_sum, up_sum = (
-        lax.psum(gate_part.astype(jnp.bfloat16), "row").astype(jnp.float32),
+        put_bands(gate_part.astype(jnp.bfloat16)).astype(jnp.float32),
         lax.psum(up_part.astype(jnp.bfloat16), "row").astype(jnp.float32),
     )
     sigmoid_gate = jax.nn.sigmoid(gate_sum)

time: 370 us -> 412 us (1.11)
  waiting for transfers between devices: 287 us -> 325 us
    all_gather x0 -> x1, waiting for transfers between devices: none -> 25.9 us  [match_block_by_axis(): taken_in = jnp.sum(lax.all_gather(shard_in, axis_name=shard_axis), 0)]
    psum x1, waiting for transfers between devices: 46.7 us -> 59.4 us  [on_device(): lax.psum(up_part.astype(jnp.bfloat16), 'row').astype(jnp.float32)]
  transfers between devices with their start and end apart: 5 -> 6, of which waited for: 5 -> 6; matrix products, arithmetic and copies ran while one was open for 4% -> 4% of each run, Pallas kernels for 0% -> 0%
where the time goes in v1:
time: 412 us; the launch traced here: 411 us
  waiting for transfers between devices  325 us (79%)
  matrix products  27.7 us (7%)
  blocking collectives  26.7 us (6%)
  between operations  14.3 us (3%)
  local copies, waits for them, and re-layouts  9.78 us (2%)
  other arithmetic  7.46 us (2%)
    all_gather x1, waiting for transfers between devices, on_device(): lax.all_gather(up_local, 'dp', axis=0, tiled=True)  71.1 us
    reduce_scatter x1, waiting for transfers between devices, on_device(): lax.psum_scatter(pair_term.astype(jnp.bfloat16), 'dp', scatter_dimension=...  67.6 us
    all_gather x1, waiting for transfers between devices, on_device(): lax.all_gather(gate_local, 'dp', axis=0, tiled=True)  61.7 us
    psum x1, waiting for transfers between devices, on_device(): lax.psum(up_part.astype(jnp.bfloat16), 'row').astype(jnp.float32)  59.4 us
    reduce_scatter x1, waiting for transfers between devices, on_device(): lax.psum_scatter(summed.reshape(tok_rows // lax.axis_size('col') * lax.ax...  37.9 us
    all_gather x1, waiting for transfers between devices, match_block_by_axis(): taken_in = jnp.sum(lax.all_gather(shard_in, axis_name=shard_axis), 0)  25.9 us
    all_gather x1, blocking collectives, on_device(): token_panel = lax.all_gather(layer_input, 'col', axis=0, tiled=True)  13.5 us
    all_gather x1, blocking collectives, on_device(): grad_panel = lax.all_gather(hidden_grad, 'row', axis=0, tiled=True)  13.2 us
  transfers between devices with their start and end apart: 6, of which 6 were waited for; matrix products, arithmetic and copies ran while one was open for 4% of the time, Pallas kernels for 0%

profile of v1, /device:TPU:8, one launch (start us, length us, event | category | flops | bytes accessed | tf_op | source)
XLA Modules:
  0.0 411.3 jit_solution(2873651495763141324)
XLA Ops:
  8.7 0.8 broadcast_compare_fusion
  10.1 13.5 %all_gather.19 = bf16[192,1024]{1,0:T(8,128)(2,1)S(1)} all-gather(bf16[24,1024]{1,0:T(8,128)(2,1)} %param.5), channel_id=1, replica_groups=mesh['dp'=16,'row'=4,'col'=8] {'col'}, dimensions={0}, use_global_device_ids=true | all-gather | bytes 442368 | tf_op jit(solution)/shard_map/all_gather | solution.py:56
  23.7 1.0 gather_fusion
  24.7 61.7 %all-gather.8.cloned.1.call-done = bf16[1,1,48,128,128]{4,3,1,0,2:T(8,128)(2,1)} async-done(((bf16[1,1,3,128,128]{4,3,1,0,2:T(8,128)(2,1)}), bf16[1,1,48,128,128]{4,3,1,0,2:T(8,128)(2,1)}) %all-gather.8.cloned.1.call-update) | async-done | bytes 1572880 | tf_op jit(solution)/shard_map/all_gather | solution.py:69
  86.4 71.1 %all-gather.10.cloned.1.call-done = bf16[1,1,48,128,128]{4,3,1,0,2:T(8,128)(2,1)} async-done(((bf16[1,1,3,128,128]{4,3,1,0,2:T(8,128)(2,1)}), bf16[1,1,48,128,128]{4,3,1,0,2:T(8,128)(2,1)}) %all-gather.10.cloned.1.call-update) | async-done | bytes 1572880 | tf_op jit(solution)/shard_map/all_gather | solution.py:70
  157.5 3.3 convolution_bitcast_fusion
  160.8 9.9 %fusion.20 = bf16[192,14,256]{2,1,0:T(8,128)(2,1)S(1)} fusion(f32[192,48,256]{2,0,1:T(8,128)S(1)} %convolution_bitcast_fusion, f32[48]{0:T(128)S(1)} %convert_element_type.64, s32[48]{0:T(128)S(1)} %get-tuple-element.6), kind=kOutput, calls=%fused_computation.23 | convolution fusion | flops 397051200 | bytes 10813824 | tf_op jit(solution)/shard_map/tsn,sc->tcn/dot_general | solution.py:40
  171.0 1.4 convert_element_type.68
  172.5 1.0 copy.54
  173.6 13.2 %all_gather.18 = bf16[192,1792]{1,0:T(8,128)(2,1)S(1)} all-gather(bf16[48,1792]{1,0:T(8,128)(2,1)S(1)} %copy-done.3), channel_id=1, replica_groups=mesh['dp'=16,'row'=4,'col'=8] {'row'}, dimensions={0}, use_global_device_ids=true | all-gather | bytes 860160 | tf_op jit(solution)/shard_map/all_gather | solution.py:57
  186.7 25.9 %all-gather.6.cloned.1.call-done = bf16[4,192,1792]{2,1,0:T(8,128)(2,1)} async-done(((bf16[1,192,1792]{2,1,0:T(8,128)(2,1)}), bf16[4,192,1792]{2,1,0:T(8,128)(2,1)}) %all-gather.6.cloned.1.call-update) | async-done | bytes 2752528 | tf_op jit(solution)/shard_map/all_gather | solution.py:9
  212.6 2.5 reduce_sum.32
  215.1 59.4 %all-reduce.2.cloned.1.call-done = bf16[192,1792]{1,0:T(8,128)(2,1)} async-done(((bf16[192,1792]{1,0:T(8,128)(2,1)}), bf16[192,1792]{1,0:T(8,128)(2,1)}) %all-reduce.2.cloned.1.call-update) | async-done | bytes 688144 | tf_op jit(solution)/shard_map/psum | solution.py:78
  274.5 1.9 fusion.36
  276.9 3.1 gather_fusion.1
  280.0 6.3 %multiply_convert_fusion = bf16[48,128,256]{2,1,0:T(8,128)(2,1)} fusion(f32[48]{0:T(128)S(1)} %convert_element_type.64, bf16[48,192,256]{2,1,0:T(8,128)(2,1)} %gather_fusion.1, pred[48]{0:T(512)(128)(4,1)S(1)} %get-tuple-element.5, bf16[48,192,128]{2,1,0:T(8,128)(2,1)} %copy-done, pred[48]{0:T(512)(128)(4,1)S(1)} %get-tuple-element.20), kind=kOutput, calls=%fused_computation.4 | convolution fusion | flops 610664448 | bytes 10223904 | tf_op jit(solution)/shard_map/tsk,tsn->skn/dot_general | solution.py:104
  286.6 1.1 copy-done.1
  288.2 3.3 fusion.10
  291.5 4.9 %fusion.32 = bf16[8,192,128]{2,0,1:T(8,128)(2,1)S(1)} fusion(f32[192,48,128]{2,0,1:T(8,128)S(1)} %fusion.10, f32[48]{0:T(128)S(1)} %convert_element_type.64, s32[48]{0:T(128)S(1)} %get-tuple-element.21), kind=kOutput, calls=%fused_computation.34 | convolution fusion | flops 113443584 | bytes 5112192 | tf_op jit(solution)/shard_map/tsk,sr->trk/dot_general | solution.py:47
  296.4 0.8 copy.57
  297.3 67.6 %reduce-scatter.5.cloned.1.call-done = bf16[3,128,256]{2,1,0:T(8,128)(2,1)} async-done(((bf16[48,128,256]{2,1,0:T(8,128)(2,1)}), bf16[3,128,256]{2,1,0:T(8,128)(2,1)}) %reduce-scatter.5.cloned.1.call-update) | async-done | bytes 196624 | tf_op jit(solution)/shard_map/reduce_scatter | solution.py:107
  364.8 1.0 convert_element_type.76
  365.8 0.8 fusion.37
  366.6 37.9 %reduce-scatter.3.cloned.1.call-done = bf16[24,1024]{1,0:T(8,128)(2,1)} async-done(((bf16[192,1024]{1,0:T(8,128)(2,1)}), bf16[24,1024]{1,0:T(8,128)(2,1)}) %reduce-scatter.3.cloned.1.call-update) | async-done | bytes 49168 | tf_op jit(solution)/shard_map/reduce_scatter | solution.py:95
  (33 shorter events, 3.8 us)
Async XLA Ops:
  7.2 79.3 %all-gather.8.cloned.1.call-start = ((), (), s32[]{:S(2)}) async-start(), calls=%async_computation.6 | async-start | bytes 1671168 | tf_op jit(solution)/shard_map/all_gather | solution.py:69
  7.9 149.6 %all-gather.10.cloned.1.call-start = ((), (), s32[]{:S(2)}) async-start(), calls=%async_computation.7 | async-start | bytes 1671168 | tf_op jit(solution)/shard_map/all_gather | solution.py:70
  8.6 203.9 %all-gather.6.cloned.1.call-start = ((), (), s32[]{:S(2)}) async-start(), calls=%async_computation.3 | async-start | bytes 3440640 | tf_op jit(solution)/shard_map/all_gather | solution.py:9
  24.7 136.1 %copy-start = (bf16[48,192,128]{2,1,0:T(8,128)(2,1)}, bf16[48,192,128]{2,1,0:T(8,128)(2,1)S(1)}, u32[]{:S(2)}) copy-start(bf16[48,192,128]{2,1,0:T(8,128)(2,1)S(1)} %gather_fusion) | copy-start | bytes 7077892
  171.0 2.5 copy-start.3
  172.4 102.1 %all-reduce.2.cloned.1.call-start = ((), (), s32[]{:S(2)}) async-start(), calls=%async_computation.2 | async-start | bytes 1376256 | tf_op jit(solution)/shard_map/psum | solution.py:78
  173.5 191.3 %reduce-scatter.5.cloned.1.call-start = ((), (), s32[]{:S(2)}) async-start(), calls=%async_computation.5 | async-start | bytes 3342336 | tf_op jit(solution)/shard_map/reduce_scatter | solution.py:107
  286.3 1.4 copy-start.1
  286.3 1.9 copy-start.2
  286.3 118.1 %reduce-scatter.3.cloned.1.call-start = ((), (), s32[]{:S(2)}) async-start(), calls=%async_computation.4 | async-start | bytes 442368 | tf_op jit(solution)/shard_map/reduce_scatter | solution.py:95
Sparse Core Ops, SparseCore 0:
  10.0 76.3 all-gather.7
  88.5 68.9 all-gather.9
  172.5 40.0 all-gather.5
  214.8 59.6 all-reduce.1
  286.4 78.3 reduce-scatter.4
  368.1 36.3 reduce-scatter.2
